TPU v7x, 128 devices: a whole 4x4x4 slice. The times are simulated.
128 devices in a mesh: seq: 16 (over z, y), tp: 8 (over x, core).
Axes of the slice: x: 4, y: 4, z: 4, core: 2. Of those that a mesh axis runs over, the one named last changes fastest.
Arguments:
- hidden: bfloat16 [128, 64, 2560], P(None, 'seq'), may hold values from -6 to 6
- gain_attn: bfloat16 [2560], replicated, may hold values from 0.099609375 to 1.8984375
- w_query: bfloat16 [2560, 2560], P(None, 'tp'), may hold values from -0.125 to 0.125
- w_key: bfloat16 [2560, 640], P(None, 'tp'), may hold values from -0.375 to 0.375
- w_value: bfloat16 [2560, 640], P(None, 'tp'), may hold values from -0.25 to 0.25
- w_out: bfloat16 [2560, 2560], P('tp'), may hold values from -0.125 to 0.125
- gain_ffn: bfloat16 [2560], replicated, may hold values from 0.099609375 to 1.8984375
- w_gate: bfloat16 [2560, 6912], P(None, 'tp'), may hold values from -0.125 to 0.125
- w_up: bfloat16 [2560, 6912], P(None, 'tp'), may hold values from -0.125 to 0.125
- w_down: bfloat16 [6912, 2560], P('tp'), may hold values from -0.078125 to 0.078125
- shared_pages: bfloat16 [320, 8, 2, 80, 128], P('seq', 'tp'), may hold values from -270 to 270
- leaf_pages: bfloat16 [512, 8, 2, 80, 128], P('seq', 'tp'), may hold values from -270 to 270
- root_table: int32 [4, 16], replicated, may hold values from 0 to 319, as said below
- mid_table: int32 [16, 16], replicated, may hold values from 0 to 319, as said below
- leaf_table: int32 [64, 8], replicated, may hold values from 0 to 511, as said below
- root_len: int32 [4], replicated, may hold values from 1024 to 2048, as said below
- mid_len: int32 [16], replicated, may hold values from 1 to 2048, as said below
- leaf_len: int32 [64], replicated, may hold values from 1 to 1024, as said below
- mid_parent: int32 [16], replicated, may hold values from 0 to 3
- leaf_parent: int32 [64], replicated, may hold values from 0 to 15
- slot_request: int32 [64], replicated, may hold values from 0 to 63, as said below
Outputs:
- layer_out: float32 [128, 64, 2560], P('tp', 'seq')
Inputs may be any that keep to these rules, and one draw needn't show every extreme that they name: `slot_request`: A permutation of the requests. The 4 requests of slots 4 * s to 4 * s + 3 have their leaves with 4 distinct owners (see leaf_table). `leaf_table`: all pages of one request's leaf lie with one owner, the index of seq equal to page // 32; each owner holds the leaves of exactly 4 requests, and every leaf page is named once. `root_table`: with mid_table, names every shared page exactly once. Shared page g is held by the index of seq g // 20; each index holds exactly 1 page of every root. `mid_table`: with root_table, names every shared page exactly once. Each index of seq holds exactly 1 page of every middle node. `root_len`: some root reaches the largest value. `mid_len`: some middle node reaches the largest value. `leaf_len`: some leaf reaches the largest value.
All inputs are finite; a program needn't handle non-finite values.
Results may differ from a plain program's by a relative error of at most 0.009.
The roundings to bfloat16 on the way count: a program that leaves them out, or rounds other values in their place, can miss the bound.
Values may be sent and summed in bfloat16 or wider, within the bound.
No kernel may reach another device: no remote copies, remote signals or barrier semaphores. Data moves between devices by JAX's collectives and lax.ppermute only.
A program may use at most 192 MiB of HBM per device.

v0:
```python
import jax
import jax.numpy as jnp
from jax import lax
from jax.sharding import PartitionSpec as P

QH = 32
KVH = 8
HD = 80
WINDOW = 4096
masked_score = -1e30
rope_base = 10000.0


def rms_norm(row_data, gain_vector):
    values = row_data.astype(jnp.float32)
    inverse_rms = lax.rsqrt(jnp.mean(values * values, -1, keepdims=True) + 1e-05)
    return (values * inverse_rms * gain_vector.astype(jnp.float32)).astype(jnp.bfloat16)


def rotate(vector, position):
    half_size = vector.shape[-1] // 2
    frequency = rope_base ** (-2.0 * jnp.arange(half_size, dtype=jnp.float32) / vector.shape[-1])
    angles = position.astype(jnp.float32)[..., None] * frequency
    cos_part = jnp.cos(angles)
    sin_part = jnp.sin(angles)
    first_half = vector[..., :half_size]
    second_half = vector[..., half_size:]
    return jnp.concatenate(
        [
            first_half * cos_part - second_half * sin_part,
            second_half * cos_part + first_half * sin_part,
        ],
        -1,
    )


def page_columns(pages):
    moved = jnp.moveaxis(pages, -5, -2)
    return moved.reshape(moved.shape[:-2] + (moved.shape[-2] * moved.shape[-1],))


def attend(queries, key_pack, key_pos, present, query_pos):
    scores = jnp.einsum(
        "nbkge,bket->nbkgt", queries, key_pack[:, :, 0], preferred_element_type=jnp.float32
    ) * queries.shape[-1] ** (-0.5)
    distance = query_pos[:, :, None] - key_pos[None, :, :]
    allowed = (present[None, :, :] & (distance >= 0) & (distance < WINDOW))[:, :, None, None, :]
    scores = jnp.where(allowed, scores, masked_score)
    maximum = jnp.max(scores, -1)
    weights = jnp.where(allowed, jnp.exp(scores - maximum[..., None]), 0.0)
    totals = jnp.sum(weights, -1)
    weighted = jnp.einsum(
        "nbkgt,bket->nbkge",
        weights.astype(jnp.bfloat16),
        key_pack[:, :, 1],
        preferred_element_type=jnp.float32,
    )
    return (weighted, maximum, totals)


def merge_parts(first, second):
    maximum = jnp.maximum(first[1], second[1])
    first_scale = jnp.exp(first[1] - maximum)
    second_scale = jnp.exp(second[1] - maximum)
    return (
        first[0] * first_scale[..., None] + second[0] * second_scale[..., None],
        maximum,
        first[2] * first_scale + second[2] * second_scale,
    )


def spans(request_ids, root_len, mid_len, leaf_len, mid_parent, leaf_parent):
    mid_nodes = leaf_parent[request_ids]
    root_nodes = mid_parent[mid_nodes]
    return (root_nodes, mid_nodes, root_len[root_nodes], mid_len[mid_nodes], leaf_len[request_ids])


def shards(
    hidden,
    gain_attn,
    w_query,
    w_key,
    w_value,
    w_out,
    gain_ffn,
    w_gate,
    w_up,
    w_down,
    shared_pages,
    leaf_pages,
    root_table,
    mid_table,
    leaf_table,
    root_len,
    mid_len,
    leaf_len,
    mid_parent,
    leaf_parent,
    slot_request,
):
    new_rows, local_reqs, model_width = hidden.shape
    seq_count = lax.axis_size("seq")
    seq_index = lax.axis_index("seq")
    kv_local = leaf_pages.shape[1]
    group_size = QH // KVH
    pages_here = leaf_pages.shape[0]
    slot_ids = seq_index * local_reqs + jnp.arange(local_reqs, dtype=jnp.int32)
    requests = slot_request[slot_ids]
    root_nodes, mid_nodes, root_span, mid_span, leaf_span = spans(
        requests, root_len, mid_len, leaf_len, mid_parent, leaf_parent
    )
    context = root_span + mid_span + leaf_span
    new_index = jnp.arange(new_rows, dtype=jnp.int32)
    query_pos = context[None, :] + new_index[:, None]
    all_slots = slot_request.reshape(seq_count, local_reqs)
    page_store = lax.all_gather(shared_pages, "seq", axis=0, tiled=True)
    root_index = root_table[root_nodes]
    mid_index = mid_table[mid_nodes]
    normed = rms_norm(hidden, gain_attn).reshape(-1, model_width)
    query_proj = jnp.dot(normed, w_query, preferred_element_type=jnp.float32).reshape(
        new_rows, local_reqs, -1, HD
    )
    queries = (
        rotate(query_proj, query_pos[:, :, None])
        .astype(jnp.bfloat16)
        .reshape(new_rows, local_reqs, kv_local, group_size, HD)
    )
    key_proj = jnp.dot(normed, w_key, preferred_element_type=jnp.float32).reshape(
        new_rows, local_reqs, kv_local, HD
    )
    new_keys = rotate(key_proj, query_pos[:, :, None]).astype(jnp.bfloat16)
    new_values = (
        jnp.dot(normed, w_value, preferred_element_type=jnp.float32)
        .astype(jnp.bfloat16)
        .reshape(new_rows, local_reqs, kv_local, HD)
    )
    home_of = leaf_table[:, 0] // pages_here
    own_homes = home_of[requests]
    sender_match = home_of[all_slots] == seq_index
    sender_pick = jnp.argmax(sender_match, 1)
    sender_have = jnp.any(sender_match, 1)
    picked_request = jnp.take_along_axis(all_slots, sender_pick[:, None], 1)[:, 0]
    page_ids = jnp.where(
        sender_have[:, None], leaf_table[picked_request] - seq_index * pages_here, 0
    )
    leaf_steps = jnp.arange(leaf_table.shape[1] * leaf_pages.shape[-1], dtype=jnp.int32)
    fresh_pack = jnp.stack(
        [jnp.transpose(new_keys, (1, 2, 3, 0)), jnp.transpose(new_values, (1, 2, 3, 0))], 2
    )
    fresh_part = attend(
        queries,
        fresh_pack,
        context[:, None] + new_index[None, :],
        jnp.ones((local_reqs, new_rows), bool),
        query_pos,
    )
    outgoing = jnp.where(
        sender_have[:, None, None, None, None, None], jnp.take(leaf_pages, page_ids, axis=0), 0
    )
    arrived = lax.all_to_all(outgoing, "seq", split_axis=0, concat_axis=0, tiled=True)
    leaf_pack = page_columns(jnp.take(arrived, own_homes, axis=0))
    leaf_pos = (root_span + mid_span)[:, None] + leaf_steps[None, :]
    leaf_part = attend(
        queries, leaf_pack, leaf_pos, leaf_steps[None, :] < leaf_span[:, None], query_pos
    )
    root_pack = page_columns(jnp.take(page_store, root_index, axis=0))
    root_steps = jnp.arange(root_pack.shape[-1], dtype=jnp.int32)
    root_part = attend(
        queries,
        root_pack,
        root_steps[None, :] + 0 * root_span[:, None],
        root_steps[None, :] < root_span[:, None],
        query_pos,
    )
    mid_pack = page_columns(jnp.take(page_store, mid_index, axis=0))
    mid_steps = jnp.arange(mid_pack.shape[-1], dtype=jnp.int32)
    mid_part = attend(
        queries,
        mid_pack,
        root_span[:, None] + mid_steps[None, :],
        mid_steps[None, :] < mid_span[:, None],
        query_pos,
    )
    combined = merge_parts(merge_parts(root_part, mid_part), merge_parts(leaf_part, fresh_part))
    attended = (
        (combined[0] / combined[2][..., None])
        .astype(jnp.bfloat16)
        .reshape(new_rows * local_reqs, -1)
    )
    attn_proj = lax.psum(jnp.dot(attended, w_out, preferred_element_type=jnp.float32), "tp")
    resid = hidden.astype(jnp.float32) + attn_proj.reshape(new_rows, local_reqs, model_width)
    normed_ffn = rms_norm(resid, gain_ffn).reshape(-1, model_width)
    gate_rows = jnp.dot(normed_ffn, w_gate, preferred_element_type=jnp.float32)
    up_rows = jnp.dot(normed_ffn, w_up, preferred_element_type=jnp.float32)
    activated = (
        (jax.nn.silu(gate_rows) * up_rows).astype(jnp.bfloat16).reshape(new_rows, local_reqs, -1)
    )
    own_count = new_rows // lax.axis_size("tp")
    ffn_proj = lax.psum_scatter(
        jnp.dot(
            activated.reshape(-1, activated.shape[-1]), w_down, preferred_element_type=jnp.float32
        ).reshape(own_count * lax.axis_size("tp"), local_reqs, model_width),
        "tp",
        scatter_dimension=0,
        tiled=True,
    )
    own_rows = lax.dynamic_slice_in_dim(resid, lax.axis_index("tp") * own_count, own_count, 0)
    return own_rows + ffn_proj


def solution(mesh):
    return jax.shard_map(
        shards,
        mesh=mesh,
        in_specs=(
            P(None, "seq", None),
            P(),
            P(None, "tp"),
            P(None, "tp"),
            P(None, "tp"),
            P("tp", None),
            P(),
            P(None, "tp"),
            P(None, "tp"),
            P("tp", None),
            P("seq", "tp", None, None, None),
            P("seq", "tp", None, None, None),
            P(),
            P(),
            P(),
            P(),
            P(),
            P(),
            P(),
            P(),
            P(),
        ),
        out_specs=P("tp", "seq", None),
        check_vma=False,
    )
```

profile of v0, /device:TPU:1, one launch (start us, length us, event | category | flops | bytes accessed | tf_op | source)
XLA Modules:
  0.0 451.2 jit_solution(16612270365806220123)
XLA Ops:
  8.8 0.8 copy.88
  10.3 0.8 gather_fusion.9
  13.6 3.6 gather_fusion.11
  17.2 5.5 %select_select_fusion = bf16[16,8,1,2,80,128]{5,4,3,1,2,0:T(8,128)(2,1)} fusion(bf16[16,8,1,2,80,128]{5,4,3,1,2,0:T(8,128)(2,1)} %bitcast.320, pred[16]{0:T(512)(128)(4,1)S(1)} %reduce_or.9, pred[16,8]{1,0:T(8,128)(4,1)S(1)} %get-tuple-element.17), kind=kLoop, calls=%fused_computation.47 | loop fusion | flops 5242880 | bytes 10485904 | tf_op jit(solution)/shard_map/jit(_where)/select_n | solution.py:157
  22.7 8.8 %all-to-all-start = ((bf16[16,8,1,2,80,128]{5,4,3,1,2,0:T(8,128)(2,1)}), bf16[16,8,1,2,80,128]{5,4,3,1,2,0:T(8,128)(2,1)}, u32[]{:S(2)}, u32[]{:S(2)}) async-start(bf16[16,8,1,2,80,128]{5,4,3,1,2,0:T(8,128)(2,1)} %select_select_fusion), calls=%async_computation | async-start | bytes 10485760 | tf_op jit(solution)/shard_map/all_to_all | solution.py:160
  37.5 3.4 fusion.17
  40.9 3.0 fusion.19
  44.0 5.8 %reshape.793 = bf16[512,2560]{1,0:T(8,128)(2,1)} reshape(bf16[128,4,2560]{2,1,0:T(4,128)(2,1)} %fusion.19) | data formatting | bytes 5242880 | tf_op jit(solution)/shard_map/reshape | solution.py:119
  49.8 2.6 convolution_convert_fusion
  52.4 0.8 copy.94
  55.5 2.8 fusion.73
  58.4 1.5 fusion.135
  60.4 1.1 fusion.30
  64.8 1.4 fusion.37
  66.5 5.5 %fusion.26 = (pred[128,4,2048]{0,2,1:T(8,128)(4,1)}, pred[128,4,2048]{0,2,1:T(8,128)(4,1)}) fusion(s32[128,4]{0,1:T(4,128)S(1)} %get-tuple-element.29, pred[4,2048]{1,0:T(4,128)(4,1)S(1)} %iota_compare_fusion.1, s32[4,2048]{1,0:T(4,128)S(1)} %iota_add_fusion, pred[4,2048]{1,0:T(4,128)(4,1)S(1)} %iota_compare_fusion), kind=kLoop, calls=%fused_computation.54 | loop fusion | flops 10485760 | bytes 2148352 | tf_op jit(solution)/shard_map/and | solution.py:47
  72.0 55.6 %all-to-all-done = bf16[16,8,1,2,80,128]{5,4,3,1,2,0:T(8,128)(2,1)} async-done(((bf16[16,8,1,2,80,128]{5,4,3,1,2,0:T(8,128)(2,1)}), bf16[16,8,1,2,80,128]{5,4,3,1,2,0:T(8,128)(2,1)}, u32[]{:S(2)}, u32[]{:S(2)}) %all-to-all-start) | async-done | bytes 5242912 | tf_op jit(solution)/shard_map/all_to_all | solution.py:160
  127.6 3.4 gather_fusion.12
  131.0 0.8 fusion.41
  132.3 1.5 reshape.788
  133.8 2.5 fusion.14
  136.3 3.2 copy-done.11
  139.7 2.7 fusion.15
  142.3 16.8 %all-gather.2.cloned.1.call-done = bf16[320,1,2,80,128]{4,3,2,1,0:T(8,128)(2,1)} async-done(((bf16[20,1,2,80,128]{4,3,2,1,0:T(8,128)(2,1)}), bf16[320,1,2,80,128]{4,3,2,1,0:T(8,128)(2,1)}) %all-gather.2.cloned.1.call-update) | async-done | bytes 13107216 | tf_op jit(solution)/shard_map/all_gather | solution.py:116
  159.2 7.1 %gather_fusion.15 = bf16[64,2,80,128]{3,2,1,0:T(8,128)(2,1)} fusion(bf16[320,2,80,128]{3,2,1,0:T(8,128)(2,1)} %bitcast.326, s32[1024]{0:T(1024)S(1)} %copy-done.31), kind=kCustom, calls=%fused_computation.1.clone | custom fusion | bytes 5243136 | tf_op jit(solution)/shard_map/jit(_take)/gather | solution.py:175
  166.2 7.2 %gather_fusion.14 = bf16[64,2,80,128]{3,2,1,0:T(8,128)(2,1)} fusion(bf16[320,2,80,128]{3,2,1,0:T(8,128)(2,1)} %bitcast.327, s32[1024]{0:T(1024)S(1)} %copy-done.30), kind=kCustom, calls=%fused_computation.clone | custom fusion | bytes 5243136 | tf_op jit(solution)/shard_map/jit(_take)/gather | solution.py:166
  173.4 4.2 fusion.35
  177.6 5.2 %reshape.777 = bf16[4,1,2,80,2048]{4,3,0,2,1:T(8,128)(2,1)} reshape(bf16[4,1,2,80,16,128]{5,4,3,0,2,1:T(8,128)(2,1)} %fusion.35) | data formatting | bytes 5242880 | tf_op jit(solution)/shard_map/reshape | solution.py:39
  182.8 4.3 fusion.34
  187.1 5.2 %reshape.781 = bf16[4,1,2,80,2048]{4,3,0,2,1:T(8,128)(2,1)} reshape(bf16[4,1,2,80,16,128]{5,4,3,0,2,1:T(8,128)(2,1)} %fusion.34) | data formatting | bytes 5242880 | tf_op jit(solution)/shard_map/reshape | solution.py:39
  192.3 8.8 %fusion.1 = (f32[128,4,4]{0,2,1:T(4,128)S(1)}, f32[4,2048,128,4]{2,1,3,0:T(8,128)}) fusion(pred[128,4,2048]{0,2,1:T(8,128)(4,1)S(1)} %copy-done.13, bf16[128,4,4,40]{0,3,2,1:T(8,128)(2,1)S(1)} %copy-done.24, bf16[128,4,4,40]{0,3,2,1:T(8,128)(2,1)S(1)} %copy-done.22, bf16[4,1,2,80,2048]{4,3,0,2,1:T(8,128)(2,1)} %reshape.781), kind=kOutput, calls=%fused_computation.21 | convolution fusion | flops 684324864 | bytes 19472384 | tf_op jit(solution)/shard_map/nbkge,bket->nbkgt/dot_general | solution.py:43
  201.1 2.7 fusion
  203.9 10.7 %fusion.2 = (f32[128,4,4]{0,2,1:T(4,128)S(1)}, f32[128,4,4]{0,2,1:T(4,128)S(1)}) fusion(f32[4,2048,128,4]{2,1,3,0:T(8,128)S(1)} %get-tuple-element.38, f32[128,4,4]{0,2,1:T(4,128)S(1)} %get-tuple-element.37, pred[128,4,2048]{0,2,1:T(8,128)(4,1)S(1)} %copy-done.12, f32[128,4,4]{0,2,1:T(4,128)S(1)} %get-tuple-element.31, ...), kind=kLoop, calls=%fused_computation.22 | loop fusion | flops 41938944 | bytes 35684352 | tf_op jit(solution)/shard_map/reduce_sum | solution.py:51
  214.7 3.0 fusion.56
  217.7 10.7 %fusion.68 = f32[128,4,1,4,80]{0,4,3,1,2:T(8,128)} fusion(f32[4,2048,128,4]{2,1,3,0:T(8,128)} %get-tuple-element.32, f32[128,4,4]{0,2,1:T(4,128)S(1)} %get-tuple-element.31, pred[128,4,2048]{0,2,1:T(8,128)(4,1)S(1)} %copy-done.13, bf16[4,1,2,80,2048]{4,3,0,2,1:T(8,128)(2,1)} %reshape.781, f32[128,4,4]{0,2,1:T(4,128)S(1)} %bitcast.342), kind=kOutput, calls=%fused_computation.94 | convolution fusion | flops 692224000 | bytes 19808256 | tf_op jit(solution)/shard_map/nbkgt,bket->nbkge/dot_general | solution.py:52
  228.4 5.8 %fusion.65 = f32[128,4,1,4,80]{0,4,3,1,2:T(8,128)} fusion(f32[128,4,1,4,80]{0,4,3,1,2:T(8,128)} %fusion.68, f32[4,2048,128,4]{2,1,3,0:T(8,128)S(1)} %get-tuple-element.38, f32[128,4,4]{0,2,1:T(4,128)S(1)} %get-tuple-element.37, pred[128,4,2048]{0,2,1:T(8,128)(4,1)S(1)} %copy-done.12, bf16[4,1,2,80,2048]{4,3,0,2,1:T(8,128)(2,1)} %reshape.777, ...), kind=kOutput, calls=%fused_computation.93 | convolution fusion | flops 692551680 | bytes 20471808 | tf_op jit(solution)/shard_map/nbkgt,bket->nbkge/dot_general | solution.py:52
  234.2 1.7 fusion.72
  236.7 3.9 fusion.123
  240.6 7.1 %reshape.798 = f32[128,4,2560]{2,1,0:T(4,128)} reshape(f32[512,2560]{1,0:T(8,128)} %fusion.123) | data formatting | bytes 10485760 | tf_op jit(solution)/shard_map/reshape | solution.py:191
  248.4 76.4 %all-reduce.4.cloned.1.call-done = f32[128,4,2560]{2,1,0:T(4,128)} async-done(((f32[128,4,2560]{2,1,0:T(4,128)}), f32[128,4,2560]{2,1,0:T(4,128)}) %all-reduce.4.cloned.1.call-update) | async-done | bytes 5242896 | tf_op jit(solution)/shard_map/psum | solution.py:190
  324.8 5.1 %multiply_reduce_fusion = (f32[128,4]{1,0:T(8,128)S(1)}, f32[128,4,2560]{2,1,0:T(4,128)S(1)}) fusion(f32[128,4,2560]{2,1,0:T(4,128)} %all-reduce.4.cloned.1.call-done, bf16[128,4,2560]{2,1,0:T(4,128)(2,1)} %param.23), kind=kLoop, calls=%fused_computation.46 | loop fusion | flops 5242368 | bytes 13109248 | tf_op jit(solution)/shard_map/reduce_sum | solution.py:16
  329.9 2.3 copy-done.9
  332.2 2.7 multiply_convert_fusion
  334.9 5.6 %reshape.799 = bf16[512,2560]{1,0:T(8,128)(2,1)} reshape(bf16[128,4,2560]{2,1,0:T(4,128)(2,1)} %multiply_convert_fusion) | data formatting | bytes 5242880 | tf_op jit(solution)/shard_map/reshape | solution.py:192
  340.5 5.5 %fusion.124 = f32[512,864]{0,1:T(8,128)S(1)} fusion(bf16[512,2560]{1,0:T(8,128)(2,1)} %reshape.799, bf16[2560,864]{0,1:T(8,128)(2,1)} %param.30), kind=kOutput, calls=%fused_computation.214 | convolution fusion | flops 2264924160 | bytes 8814592 | tf_op jit(solution)/shard_map/dot_general | solution.py:193
  346.0 12.0 %fusion.78 = f32[512,2560]{1,0:T(8,128)} fusion(bf16[864,2560]{1,0:T(8,128)(2,1)} %param.32, f32[512,864]{0,1:T(8,128)S(1)} %fusion.124, bf16[512,2560]{1,0:T(8,128)(2,1)} %reshape.799, bf16[2560,864]{0,1:T(8,128)(2,1)} %param.31), kind=kOutput, calls=%fused_computation.102 | convolution fusion | flops 4532502528 | bytes 18481152 | tf_op jit(solution)/shard_map/dot_general | solution.py:200
  358.1 7.1 %reshape.800 = f32[128,4,2560]{2,1,0:T(4,128)} reshape(f32[512,2560]{1,0:T(8,128)} %fusion.78) | data formatting | bytes 10485760 | tf_op jit(solution)/shard_map/reshape | solution.py:202
  367.1 75.0 %all-reduce.6.cloned.1.call-done = f32[128,4,2560]{2,1,0:T(4,128)} async-done(((f32[128,4,2560]{2,1,0:T(4,128)}), f32[128,4,2560]{2,1,0:T(4,128)}) %all-reduce.6.cloned.1.call-update) | async-done | bytes 5242896
  442.1 2.3 dynamic-slice_add_fusion
  (163 shorter events, 21.2 us)
Async XLA Ops:
  6.5 230.2 %copy-start = (bf16[320,2560]{1,0:T(8,128)(2,1)S(1)}, bf16[320,2560]{1,0:T(8,128)(2,1)}, u32[]{:S(2)}) copy-start(bf16[320,2560]{1,0:T(8,128)(2,1)} %param.28) | copy-start | bytes 4915204
  6.5 152.6 %all-gather.2.cloned.1.call-start = ((), (), s32[]{:S(2)}) async-start(), calls=%async_computation.1 | async-start | bytes 13926400 | tf_op jit(solution)/shard_map/all_gather | solution.py:116
  10.3 3.3 copy-start.10
  22.7 9.0 %copy-start.1 = (s32[64]{0:T(128)S(1)}, s32[64]{0:T(128)}, u32[]{:S(2)}) copy-start(s32[64]{0:T(128)} %param.43) | copy-start | bytes 772
  22.7 10.3 %copy-start.2 = (s32[64]{0:T(128)S(1)}, s32[64]{0:T(128)}, u32[]{:S(2)}) copy-start(s32[64]{0:T(128)} %param.40) | copy-start | bytes 772
  22.7 10.9 %copy-start.3 = (s32[64]{0:T(128)S(1)}, s32[64]{0:T(128)}, u32[]{:S(2)}) copy-start(s32[64]{0:T(128)} %param.42) | copy-start | bytes 772
  22.7 11.6 %copy-start.4 = (s32[16]{0:T(128)S(1)}, s32[16]{0:T(128)}, u32[]{:S(2)}) copy-start(s32[16]{0:T(128)} %param.39) | copy-start | bytes 196
  22.7 12.2 %copy-start.5 = (s32[16]{0:T(128)S(1)}, s32[16]{0:T(128)}, u32[]{:S(2)}) copy-start(s32[16]{0:T(128)} %param.41) | copy-start | bytes 196
  22.7 12.9 %copy-start.26 = (s32[16,16]{1,0:T(8,128)S(1)}, s32[16,16]{1,0:T(8,128)}, u32[]{:S(2)}) copy-start(s32[16,16]{1,0:T(8,128)} %param.36) | copy-start | bytes 3076
  22.7 13.5 %copy-start.6 = (s32[4]{0:T(128)S(1)}, s32[4]{0:T(128)}, u32[]{:S(2)}) copy-start(s32[4]{0:T(128)} %param.38) | copy-start | bytes 52
  22.7 14.2 %copy-start.25 = (s32[4,16]{1,0:T(4,128)S(1)}, s32[4,16]{1,0:T(4,128)}, u32[]{:S(2)}) copy-start(s32[4,16]{1,0:T(4,128)} %param.35) | copy-start | bytes 772
  22.7 14.8 %copy-start.32 = (bf16[2560]{0:T(1024)(128)(2,1)S(1)}, bf16[2560]{0:T(1024)(128)(2,1)}, u32[]{:S(2)}) copy-start(bf16[2560]{0:T(1024)(128)(2,1)} %param.24) | copy-start | bytes 15364
  22.7 104.8 %all-to-all-start = ((bf16[16,8,1,2,80,128]{5,4,3,1,2,0:T(8,128)(2,1)}), bf16[16,8,1,2,80,128]{5,4,3,1,2,0:T(8,128)(2,1)}, u32[]{:S(2)}, u32[]{:S(2)}) async-start(bf16[16,8,1,2,80,128]{5,4,3,1,2,0:T(8,128)(2,1)} %select_select_fusion), calls=%async_computation | async-start | bytes 10485760 | tf_op jit(solution)/shard_map/all_to_all | solution.py:160
  31.6 293.2 %all-reduce.4.cloned.1.call-start = ((), (), s32[]{:S(2)}) async-start(), calls=%async_computation.2 | async-start | bytes 10485760 | tf_op jit(solution)/shard_map/psum | solution.py:190
  37.5 3.4 copy-start.7
  40.9 8.9 %copy-start.20 = (bf16[2560,80]{0,1:T(8,128)(2,1)S(1)}, bf16[2560,80]{0,1:T(8,128)(2,1)}, u32[]{:S(2)}) copy-start(bf16[2560,80]{0,1:T(8,128)(2,1)} %param.27) | copy-start | bytes 1228804
  44.0 11.6 %copy-start.37 = (bf16[2560,80]{0,1:T(8,128)(2,1)S(1)}, bf16[2560,80]{0,1:T(8,128)(2,1)}, u32[]{:S(2)}) copy-start(bf16[2560,80]{0,1:T(8,128)(2,1)} %param.26) | copy-start | bytes 1228804
  53.2 5.2 %copy-start.8 = (bf16[128,4,2560]{2,1,0:T(4,128)(2,1)S(1)}, bf16[128,4,2560]{2,1,0:T(4,128)(2,1)}, u32[]{:S(2)}) copy-start(bf16[128,4,2560]{2,1,0:T(4,128)(2,1)} %param.23) | copy-start | bytes 7864324
  55.5 4.9 %copy-start.36 = (bf16[2560,320]{0,1:T(8,128)(2,1)S(1)}, bf16[2560,320]{0,1:T(8,128)(2,1)}, u32[]{:S(2)}) copy-start(bf16[2560,320]{0,1:T(8,128)(2,1)} %param.25) | copy-start | bytes 4915204
  61.6 0.7 copy-start.21
  61.6 1.0 copy-start.23
  62.7 2.1 copy-start.18
  66.2 70.1 %copy-start.15 = (pred[128,4,1024]{0,2,1:T(8,128)(4,1)}, pred[128,4,1024]{0,2,1:T(8,128)(4,1)S(1)}, u32[]{:S(2)}) copy-start(pred[128,4,1024]{0,2,1:T(8,128)(4,1)S(1)} %fusion.37) | copy-start | bytes 1572868
  136.3 3.2 copy-start.11
  136.3 3.3 copy-start.27
  139.7 19.5 %copy-start.31 = (s32[1024]{0:T(1024)S(1)}, s32[1024]{0:T(1024)}, u32[]{:S(2)}) copy-start(s32[1024]{0:T(1024)} %pad_clamp_fusion.4) | copy-start | bytes 12292
  142.3 23.9 %copy-start.30 = (s32[1024]{0:T(1024)S(1)}, s32[1024]{0:T(1024)}, u32[]{:S(2)}) copy-start(s32[1024]{0:T(1024)} %pad_clamp_fusion.5) | copy-start | bytes 12292
  159.2 14.3 %copy-start.35 = (pred[4,16]{1,0:T(4,128)(4,1)S(1)}, pred[4,16]{1,0:T(4,128)(4,1)}, u32[]{:S(2)}) copy-start(pred[4,16]{1,0:T(4,128)(4,1)} %compare_and_fusion.2) | copy-start | bytes 196
  173.4 9.4 %copy-start.34 = (pred[4,16]{1,0:T(4,128)(4,1)S(1)}, pred[4,16]{1,0:T(4,128)(4,1)}, u32[]{:S(2)}) copy-start(pred[4,16]{1,0:T(4,128)(4,1)} %compare_and_fusion.1) | copy-start | bytes 196
  182.8 9.5 %copy-start.13 = (pred[128,4,2048]{0,2,1:T(8,128)(4,1)S(1)}, pred[128,4,2048]{0,2,1:T(8,128)(4,1)}, u32[]{:S(2)}) copy-start(pred[128,4,2048]{0,2,1:T(8,128)(4,1)} %get-tuple-element.28) | copy-start | bytes 3145732
  182.8 9.5 %copy-start.22 = (bf16[128,4,4,40]{0,3,2,1:T(8,128)(2,1)S(1)}, bf16[128,4,4,40]{0,3,2,1:T(8,128)(2,1)}, u32[]{:S(2)}) copy-start(bf16[128,4,4,40]{0,3,2,1:T(8,128)(2,1)} %copy-done.21) | copy-start | bytes 491524
  182.8 9.5 %copy-start.24 = (bf16[128,4,4,40]{0,3,2,1:T(8,128)(2,1)S(1)}, bf16[128,4,4,40]{0,3,2,1:T(8,128)(2,1)}, u32[]{:S(2)}) copy-start(bf16[128,4,4,40]{0,3,2,1:T(8,128)(2,1)} %copy-done.23) | copy-start | bytes 491524
  192.3 8.8 %copy-start.12 = (pred[128,4,2048]{0,2,1:T(8,128)(4,1)S(1)}, pred[128,4,2048]{0,2,1:T(8,128)(4,1)}, u32[]{:S(2)}) copy-start(pred[128,4,2048]{0,2,1:T(8,128)(4,1)} %get-tuple-element.27) | copy-start | bytes 3145732
  192.3 8.8 %copy-start.14 = (bf16[4,1,2,80,2048]{4,3,0,2,1:T(8,128)(2,1)S(1)}, bf16[4,1,2,80,2048]{4,3,0,2,1:T(8,128)(2,1)}, u32[]{:S(2)}) copy-start(bf16[4,1,2,80,2048]{4,3,0,2,1:T(8,128)(2,1)} %reshape.777) | copy-start | bytes 7864324
  201.1 13.6 %slice-start = ((s8[8388608]{0:T(1024)(128)(4,1)}), s8[4194304]{0:T(1024)(128)(4,1)S(1)}, s32[]{:S(2)}) async-start(s8[8388608]{0:T(1024)(128)(4,1)} %bitcast.324), calls=%async_computation.4 | async-start | bytes 8388608
  203.9 10.8 %copy-start.28 = (f32[128,4,4]{0,2,1:T(4,128)S(1)}, f32[128,4,4]{0,2,1:T(4,128)}, u32[]{:S(2)}) copy-start(f32[128,4,4]{0,2,1:T(4,128)} %copy-done.27) | copy-start | bytes 24580
  203.9 10.8 %copy-start.29 = (f32[128,4,4]{0,2,1:T(4,128)S(1)}, f32[128,4,4]{0,2,1:T(4,128)}, u32[]{:S(2)}) copy-start(f32[128,4,4]{0,2,1:T(4,128)} %fusion.15) | copy-start | bytes 24580
  203.9 10.8 %slice-start.1 = ((s8[8388608]{0:T(1024)(128)(4,1)}), s8[4194304]{0:T(1024)(128)(4,1)S(1)}, s32[]{:S(2)}) async-start(s8[8388608]{0:T(1024)(128)(4,1)} %bitcast.324), calls=%async_computation.5 | async-start | bytes 8388608
  203.9 10.8 %copy-start.16 = (pred[128,4,1024]{0,2,1:T(8,128)(4,1)S(1)}, pred[128,4,1024]{0,2,1:T(8,128)(4,1)}, u32[]{:S(2)}) copy-start(pred[128,4,1024]{0,2,1:T(8,128)(4,1)} %copy-done.15) | copy-start | bytes 1572868
  203.9 10.8 %copy-start.17 = (bf16[4,1,2,80,1024]{4,3,0,2,1:T(8,128)(2,1)S(1)}, bf16[4,1,2,80,1024]{4,3,0,2,1:T(8,128)(2,1)}, u32[]{:S(2)}) copy-start(bf16[4,1,2,80,1024]{4,3,0,2,1:T(8,128)(2,1)} %reshape.788) | copy-start | bytes 3932164
  228.4 5.8 %copy-start.19 = (f32[128,4,1,4,128]{0,4,3,1,2:T(8,128)S(1)}, f32[128,4,1,4,128]{0,4,3,1,2:T(8,128)}, u32[]{:S(2)}) copy-start(f32[128,4,1,4,128]{0,4,3,1,2:T(8,128)} %copy-done.18) | copy-start | bytes 3145732
  247.7 0.7 copy-start.33
  247.7 194.3 %all-reduce.6.cloned.1.call-start = ((), (), s32[]{:S(2)}) async-start(), calls=%async_computation.3 | async-start | bytes 10485760
  329.9 2.3 copy-start.9
  365.2 0.7 copy-start.38
Sparse Core Ops, SparseCore 0:
  9.5 149.6 all-gather.1
  247.8 76.8 all-reduce.3
  365.3 76.6 all-reduce.5
where the time goes:
time: 457 us; the launch traced here: 451 us
  waiting for transfers between devices  225 us (49%)
  local copies, waits for them, and re-layouts  79.4 us (17%)
  matrix products  63.6 us (14%)
  other arithmetic  60 us (13%)
  between operations  14.6 us (3%)
  starting transfers between devices  8.91 us (2%)
    psum x1, waiting for transfers between devices, shards(): lax.psum(jnp.dot(attended, w_out, preferred_element_type=jnp.float32), 'tp')  76.4 us
    unnamed x4, waiting for transfers between devices  75.7 us
    all_to_all x1, waiting for transfers between devices, shards(): lax.all_to_all(outgoing, 'seq', split_axis=0, concat_axis=0, tiled=True)  55.6 us
    dot_general x4, matrix products, attend(): jnp.einsum('nbkgt,bket->nbkge', weights.astype(jnp.bfloat16), key_pack[:,...  21.1 us
    all_gather x1, waiting for transfers between devices, shards(): page_store = lax.all_gather(shared_pages, 'seq', axis=0, tiled=True)  16.8 us
    dot_general x4, matrix products, attend(): jnp.einsum('nbkge,bket->nbkgt', queries, key_pack[:, :, 0], preferred_ele...  14.5 us
    reduce_sum x3, other arithmetic, attend(): totals = jnp.sum(weights, -1)  13.6 us
    dot_general x1, matrix products, shards(): jnp.dot(activated.reshape(-1, activated.shape[-1]), w_down, preferred_ele...  12 us
  transfers between devices with their start and end apart: 4, of which 4 were waited for; matrix products, arithmetic and copies ran while one was open for 15% of the time, Pallas kernels for 0%

commit v1 on v0

--- a/solution.py
+++ b/solution.py
@@ -113,7 +113,9 @@
     new_index = jnp.arange(new_rows, dtype=jnp.int32)
     query_pos = context[None, :] + new_index[:, None]
     all_slots = slot_request.reshape(seq_count, local_reqs)
-    page_store = lax.all_gather(shared_pages, "seq", axis=0, tiled=True)
+    page_store = jnp.concatenate(
+        lax.all_to_all(jnp.stack([shared_pages] * lax.axis_size("seq")), "seq", 0, 0), axis=0
+    )
     root_index = root_table[root_nodes]
     mid_index = mid_table[mid_nodes]
     normed = rms_norm(hidden, gain_attn).reshape(-1, model_width)

time: 457 us -> 613 us (1.34)
  waiting for transfers between devices: 225 us -> 366 us
  local copies, waits for them, and re-layouts: 79.4 us -> 91.3 us
    all_to_all x0 -> x1, waiting for transfers between devices: none -> 136 us  [shards(): lax.all_to_all(jnp.stack([shared_pages] * lax.axis_size('seq')), 'seq', 0...]
    all_to_all x1, waiting for transfers between devices: 55.6 us -> 76.6 us  [shards(): lax.all_to_all(outgoing, 'seq', split_axis=0, concat_axis=0, tiled=True)]
    all_gather x1 -> x0, waiting for transfers between devices: 16.8 us -> none  [shards(): page_store = lax.all_gather(shared_pages, 'seq', axis=0, tiled=True)]
    another operation x0 -> x1, local copies, waits for them, and re-layouts: none -> 7.28 us  [shards(): jnp.stack([shared_pages] * lax.axis_size('seq'))]
    unnamed x4 -> x3, waiting for transfers between devices: 75.7 us -> 75 us
  transfers between devices with their start and end apart: 4 -> 4, of which waited for: 4 -> 4; matrix products, arithmetic and copies ran while one was open for 15% -> 8% of each run, Pallas kernels for 0% -> 0%
where the time goes in v1:
time: 613 us; the launch traced here: 605 us
  waiting for transfers between devices  366 us (60%)
  local copies, waits for them, and re-layouts  91.3 us (15%)
  matrix products  63.8 us (10%)
  other arithmetic  55.4 us (9%)
  between operations  14.9 us (2%)
  starting transfers between devices  14.1 us (2%)
    all_to_all x1, waiting for transfers between devices, shards(): lax.all_to_all(jnp.stack([shared_pages] * lax.axis_size('seq')), 'seq', 0...  136 us
    psum x1, waiting for transfers between devices, shards(): lax.psum(jnp.dot(attended, w_out, preferred_element_type=jnp.float32), 'tp')  78.5 us
    all_to_all x1, waiting for transfers between devices, shards(): lax.all_to_all(outgoing, 'seq', split_axis=0, concat_axis=0, tiled=True)  76.6 us
    unnamed x3, waiting for transfers between devices  75 us
    dot_general x4, matrix products, attend(): jnp.einsum('nbkgt,bket->nbkge', weights.astype(jnp.bfloat16), key_pack[:,...  21.3 us
    dot_general x4, matrix products, attend(): jnp.einsum('nbkge,bket->nbkgt', queries, key_pack[:, :, 0], preferred_ele...  14.4 us
    reduce_sum x3, other arithmetic, attend(): totals = jnp.sum(weights, -1)  13.6 us
  transfers between devices with their start and end apart: 4, of which 4 were waited for; matrix products, arithmetic and copies ran while one was open for 8% of the time, Pallas kernels for 0%

profile of v1, /device:TPU:1, one launch (start us, length us, event | category | flops | bytes accessed | tf_op | source)
XLA Modules:
  0.0 605.1 jit_solution(15854048872325286427)
XLA Ops:
  13.0 3.6 gather_fusion.11
  16.6 5.5 select_select_fusion
  22.1 8.8 %all-to-all-start.1 = ((bf16[16,8,1,2,80,128]{5,4,3,1,2,0:T(8,128)(2,1)}), bf16[16,8,1,2,80,128]{5,4,3,1,2,0:T(8,128)(2,1)}, u32[]{:S(2)}, u32[]{:S(2)}) async-start(bf16[16,8,1,2,80,128]{5,4,3,1,2,0:T(8,128)(2,1)} %select_select_fusion), calls=%async_computation.1 | async-start | bytes 10485760 | tf_op jit(solution)/shard_map/all_to_all | solution.py:162
  31.6 76.6 %all-to-all-done.1 = bf16[16,8,1,2,80,128]{5,4,3,1,2,0:T(8,128)(2,1)} async-done(((bf16[16,8,1,2,80,128]{5,4,3,1,2,0:T(8,128)(2,1)}), bf16[16,8,1,2,80,128]{5,4,3,1,2,0:T(8,128)(2,1)}, u32[]{:S(2)}, u32[]{:S(2)}) %all-to-all-start.1) | async-done | bytes 5242912 | tf_op jit(solution)/shard_map/all_to_all | solution.py:162
  108.2 7.3 %stack.2 = bf16[16,20,1,2,80,128]{5,4,3,2,1,0:T(8,128)(2,1)} broadcast(bf16[20,2,80,128]{3,2,1,0:T(8,128)(2,1)S(1)} %bitcast.329), dimensions={1,3,4,5} | broadcast | bytes 13926400 | tf_op jit(solution)/shard_map/stack | solution.py:117
  115.6 5.2 all-to-all-start
  126.1 3.3 fusion.17
  129.4 3.0 fusion.19
  132.4 5.5 reshape.800
  137.9 2.6 convolution_convert_fusion
  143.8 2.8 fusion.71
  147.0 1.5 fusion.133
  148.5 1.1 fusion.30
  152.7 1.4 fusion.35
  154.4 5.5 fusion.26
  159.9 3.4 gather_fusion.12
  164.6 1.4 reshape.795
  166.0 2.5 fusion.14
  168.6 3.2 copy-done.11
  171.8 2.7 fusion.15
  174.5 135.5 %all-to-all-done = bf16[16,20,1,2,80,128]{5,4,3,2,1,0:T(8,128)(2,1)} async-done(((bf16[16,20,1,2,80,128]{5,4,3,2,1,0:T(8,128)(2,1)}), bf16[16,20,1,2,80,128]{5,4,3,2,1,0:T(8,128)(2,1)}, u32[]{:S(2)}, u32[]{:S(2)}) %all-to-all-start) | async-done | bytes 13107232 | tf_op jit(solution)/shard_map/all_to_all | solution.py:117
  310.0 7.1 %gather_fusion.15 = bf16[64,2,80,128]{3,2,1,0:T(8,128)(2,1)} fusion(bf16[320,2,80,128]{3,2,1,0:T(8,128)(2,1)} %bitcast.9, s32[1024]{0:T(1024)S(1)} %copy-done.32), kind=kCustom, calls=%fused_computation.1.clone | custom fusion | bytes 5243136 | tf_op jit(solution)/shard_map/jit(_take)/gather | solution.py:177
  317.1 7.1 %gather_fusion.14 = bf16[64,2,80,128]{3,2,1,0:T(8,128)(2,1)} fusion(bf16[320,2,80,128]{3,2,1,0:T(8,128)(2,1)} %bitcast.9, s32[1024]{0:T(1024)S(1)} %copy-done.31), kind=kCustom, calls=%fused_computation.clone | custom fusion | bytes 5243136 | tf_op jit(solution)/shard_map/jit(_take)/gather | solution.py:168
  324.2 2.0 select_bitcast_fusion.1
  326.3 2.5 copy.79
  328.8 5.2 reshape.784
  334.0 2.0 select_bitcast_fusion
  336.1 2.5 copy.84
  338.6 5.2 reshape.788
  343.8 8.8 %fusion.1 = (f32[128,4,4]{0,2,1:T(4,128)S(1)}, f32[4,2048,128,4]{2,1,3,0:T(8,128)}) fusion(pred[128,4,2048]{0,2,1:T(8,128)(4,1)S(1)} %copy-done.13, bf16[128,4,4,40]{0,3,2,1:T(8,128)(2,1)S(1)} %copy-done.25, bf16[128,4,4,40]{0,3,2,1:T(8,128)(2,1)S(1)} %copy-done.23, bf16[4,1,2,80,2048]{4,3,0,2,1:T(8,128)(2,1)} %reshape.788), kind=kOutput, calls=%fused_computation.21 | convolution fusion | flops 684324864 | bytes 19472384 | tf_op jit(solution)/shard_map/nbkge,bket->nbkgt/dot_general | solution.py:43
  352.6 2.7 fusion
  355.4 10.7 %fusion.2 = (f32[128,4,4]{0,2,1:T(4,128)S(1)}, f32[128,4,4]{0,2,1:T(4,128)S(1)}) fusion(f32[4,2048,128,4]{2,1,3,0:T(8,128)S(1)} %get-tuple-element.38, f32[128,4,4]{0,2,1:T(4,128)S(1)} %get-tuple-element.37, pred[128,4,2048]{0,2,1:T(8,128)(4,1)S(1)} %copy-done.12, f32[128,4,4]{0,2,1:T(4,128)S(1)} %get-tuple-element.31, ...), kind=kLoop, calls=%fused_computation.22 | loop fusion | flops 41938944 | bytes 35684352 | tf_op jit(solution)/shard_map/reduce_sum | solution.py:51
  366.2 3.2 fusion.54
  369.4 10.7 %fusion.66 = f32[128,4,1,4,80]{0,4,3,1,2:T(8,128)} fusion(f32[4,2048,128,4]{2,1,3,0:T(8,128)} %get-tuple-element.32, f32[128,4,4]{0,2,1:T(4,128)S(1)} %get-tuple-element.31, pred[128,4,2048]{0,2,1:T(8,128)(4,1)S(1)} %copy-done.13, bf16[4,1,2,80,2048]{4,3,0,2,1:T(8,128)(2,1)} %reshape.788, f32[128,4,4]{0,2,1:T(4,128)S(1)} %bitcast.344), kind=kOutput, calls=%fused_computation.92 | convolution fusion | flops 692224000 | bytes 19808256 | tf_op jit(solution)/shard_map/nbkgt,bket->nbkge/dot_general | solution.py:52
  380.1 5.8 fusion.63
  385.9 1.7 fusion.70
  388.4 3.9 fusion.121
  392.3 7.1 %reshape.805 = f32[128,4,2560]{2,1,0:T(4,128)} reshape(f32[512,2560]{1,0:T(8,128)} %fusion.121) | data formatting | bytes 10485760 | tf_op jit(solution)/shard_map/reshape | solution.py:193
  400.1 78.5 %all-reduce.4.cloned.1.call-done = f32[128,4,2560]{2,1,0:T(4,128)} async-done(((f32[128,4,2560]{2,1,0:T(4,128)}), f32[128,4,2560]{2,1,0:T(4,128)}) %all-reduce.4.cloned.1.call-update) | async-done | bytes 5242896 | tf_op jit(solution)/shard_map/psum | solution.py:192
  478.6 5.1 multiply_reduce_fusion
  483.7 2.3 copy-done.9
  486.0 2.7 multiply_convert_fusion
  488.8 5.5 reshape.806
  494.3 5.5 fusion.122
  499.8 12.0 %fusion.76 = f32[512,2560]{1,0:T(8,128)} fusion(bf16[864,2560]{1,0:T(8,128)(2,1)} %param.32, f32[512,864]{0,1:T(8,128)S(1)} %fusion.122, bf16[512,2560]{1,0:T(8,128)(2,1)} %reshape.806, bf16[2560,864]{0,1:T(8,128)(2,1)} %param.31), kind=kOutput, calls=%fused_computation.100 | convolution fusion | flops 4532502528 | bytes 18481152 | tf_op jit(solution)/shard_map/dot_general | solution.py:202
  511.8 7.1 %reshape.807 = f32[128,4,2560]{2,1,0:T(4,128)} reshape(f32[512,2560]{1,0:T(8,128)} %fusion.76) | data formatting | bytes 10485760 | tf_op jit(solution)/shard_map/reshape | solution.py:204
  520.9 74.9 %all-reduce.6.cloned.1.call-done = f32[128,4,2560]{2,1,0:T(4,128)} async-done(((f32[128,4,2560]{2,1,0:T(4,128)}), f32[128,4,2560]{2,1,0:T(4,128)}) %all-reduce.6.cloned.1.call-update) | async-done | bytes 5242896
  595.8 2.3 dynamic-slice_add_fusion
  (167 shorter events, 23.4 us)
Async XLA Ops:
  6.5 381.8 %copy-start = (bf16[320,2560]{1,0:T(8,128)(2,1)S(1)}, bf16[320,2560]{1,0:T(8,128)(2,1)}, u32[]{:S(2)}) copy-start(bf16[320,2560]{1,0:T(8,128)(2,1)} %param.28) | copy-start | bytes 4915204
  9.7 3.3 copy-start.10
  22.1 8.8 %copy-start.1 = (s32[64]{0:T(128)S(1)}, s32[64]{0:T(128)}, u32[]{:S(2)}) copy-start(s32[64]{0:T(128)} %param.43) | copy-start | bytes 772
  22.1 86.1 %copy-start.20 = (bf16[20,1,2,80,128]{4,3,2,1,0:T(8,128)(2,1)S(1)}, bf16[20,1,2,80,128]{4,3,2,1,0:T(8,128)(2,1)}, u32[]{:S(2)}) copy-start(bf16[20,1,2,80,128]{4,3,2,1,0:T(8,128)(2,1)} %param.33) | copy-start | bytes 2457604
  22.1 86.1 %all-to-all-start.1 = ((bf16[16,8,1,2,80,128]{5,4,3,1,2,0:T(8,128)(2,1)}), bf16[16,8,1,2,80,128]{5,4,3,1,2,0:T(8,128)(2,1)}, u32[]{:S(2)}, u32[]{:S(2)}) async-start(bf16[16,8,1,2,80,128]{5,4,3,1,2,0:T(8,128)(2,1)} %select_select_fusion), calls=%async_computation.1 | async-start | bytes 10485760 | tf_op jit(solution)/shard_map/all_to_all | solution.py:162
  115.5 6.0 copy-start.2
  115.5 6.6 %copy-start.3 = (s32[64]{0:T(128)S(1)}, s32[64]{0:T(128)}, u32[]{:S(2)}) copy-start(s32[64]{0:T(128)} %param.42) | copy-start | bytes 772
  115.5 7.3 %copy-start.4 = (s32[16]{0:T(128)S(1)}, s32[16]{0:T(128)}, u32[]{:S(2)}) copy-start(s32[16]{0:T(128)} %param.39) | copy-start | bytes 196
  115.5 7.9 %copy-start.5 = (s32[16]{0:T(128)S(1)}, s32[16]{0:T(128)}, u32[]{:S(2)}) copy-start(s32[16]{0:T(128)} %param.41) | copy-start | bytes 196
  115.5 8.6 %copy-start.27 = (s32[16,16]{1,0:T(8,128)S(1)}, s32[16,16]{1,0:T(8,128)}, u32[]{:S(2)}) copy-start(s32[16,16]{1,0:T(8,128)} %param.36) | copy-start | bytes 3076
  115.5 9.2 %copy-start.6 = (s32[4]{0:T(128)S(1)}, s32[4]{0:T(128)}, u32[]{:S(2)}) copy-start(s32[4]{0:T(128)} %param.38) | copy-start | bytes 52
  115.5 9.9 %copy-start.26 = (s32[4,16]{1,0:T(4,128)S(1)}, s32[4,16]{1,0:T(4,128)}, u32[]{:S(2)}) copy-start(s32[4,16]{1,0:T(4,128)} %param.35) | copy-start | bytes 772
  115.6 10.5 %copy-start.33 = (bf16[2560]{0:T(1024)(128)(2,1)S(1)}, bf16[2560]{0:T(1024)(128)(2,1)}, u32[]{:S(2)}) copy-start(bf16[2560]{0:T(1024)(128)(2,1)} %param.24) | copy-start | bytes 15364
  115.6 194.5 %all-to-all-start = ((bf16[16,20,1,2,80,128]{5,4,3,2,1,0:T(8,128)(2,1)}), bf16[16,20,1,2,80,128]{5,4,3,2,1,0:T(8,128)(2,1)}, u32[]{:S(2)}, u32[]{:S(2)}) async-start(bf16[16,20,1,2,80,128]{5,4,3,2,1,0:T(8,128)(2,1)} %stack.2), calls=%async_computation | async-start | bytes 26214400 | tf_op jit(solution)/shard_map/all_to_all | solution.py:117
  120.8 357.8 %all-reduce.4.cloned.1.call-start = ((), (), s32[]{:S(2)}) async-start(), calls=%async_computation.2 | async-start | bytes 10485760 | tf_op jit(solution)/shard_map/psum | solution.py:192
  126.1 3.4 copy-start.7
  129.4 8.5 %copy-start.21 = (bf16[2560,80]{0,1:T(8,128)(2,1)S(1)}, bf16[2560,80]{0,1:T(8,128)(2,1)}, u32[]{:S(2)}) copy-start(bf16[2560,80]{0,1:T(8,128)(2,1)} %param.27) | copy-start | bytes 1228804
  132.4 11.3 %copy-start.38 = (bf16[2560,80]{0,1:T(8,128)(2,1)S(1)}, bf16[2560,80]{0,1:T(8,128)(2,1)}, u32[]{:S(2)}) copy-start(bf16[2560,80]{0,1:T(8,128)(2,1)} %param.26) | copy-start | bytes 1228804
  141.3 5.7 copy-start.8
  143.8 4.7 copy-start.37
  149.7 0.7 copy-start.22
  149.7 1.0 copy-start.24
  150.7 1.9 copy-start.18
  154.1 14.5 %copy-start.15 = (pred[128,4,1024]{0,2,1:T(8,128)(4,1)}, pred[128,4,1024]{0,2,1:T(8,128)(4,1)S(1)}, u32[]{:S(2)}) copy-start(pred[128,4,1024]{0,2,1:T(8,128)(4,1)S(1)} %fusion.35) | copy-start | bytes 1572868
  168.6 3.3 copy-start.11
  168.6 3.3 copy-start.28
  171.8 138.2 %copy-start.32 = (s32[1024]{0:T(1024)S(1)}, s32[1024]{0:T(1024)}, u32[]{:S(2)}) copy-start(s32[1024]{0:T(1024)} %pad_clamp_fusion.4) | copy-start | bytes 12292
  174.5 142.6 %copy-start.31 = (s32[1024]{0:T(1024)S(1)}, s32[1024]{0:T(1024)}, u32[]{:S(2)}) copy-start(s32[1024]{0:T(1024)} %pad_clamp_fusion.5) | copy-start | bytes 12292
  310.0 14.2 %copy-start.36 = (pred[4,16]{1,0:T(4,128)(4,1)S(1)}, pred[4,16]{1,0:T(4,128)(4,1)}, u32[]{:S(2)}) copy-start(pred[4,16]{1,0:T(4,128)(4,1)} %compare_and_fusion.2) | copy-start | bytes 196
  326.3 7.7 %copy-start.35 = (pred[4,16]{1,0:T(4,128)(4,1)S(1)}, pred[4,16]{1,0:T(4,128)(4,1)}, u32[]{:S(2)}) copy-start(pred[4,16]{1,0:T(4,128)(4,1)} %compare_and_fusion.1) | copy-start | bytes 196
  336.0 7.7 %copy-start.13 = (pred[128,4,2048]{0,2,1:T(8,128)(4,1)S(1)}, pred[128,4,2048]{0,2,1:T(8,128)(4,1)}, u32[]{:S(2)}) copy-start(pred[128,4,2048]{0,2,1:T(8,128)(4,1)} %get-tuple-element.28) | copy-start | bytes 3145732
  336.1 7.7 %copy-start.23 = (bf16[128,4,4,40]{0,3,2,1:T(8,128)(2,1)S(1)}, bf16[128,4,4,40]{0,3,2,1:T(8,128)(2,1)}, u32[]{:S(2)}) copy-start(bf16[128,4,4,40]{0,3,2,1:T(8,128)(2,1)} %copy-done.22) | copy-start | bytes 491524
  336.1 7.7 %copy-start.25 = (bf16[128,4,4,40]{0,3,2,1:T(8,128)(2,1)S(1)}, bf16[128,4,4,40]{0,3,2,1:T(8,128)(2,1)}, u32[]{:S(2)}) copy-start(bf16[128,4,4,40]{0,3,2,1:T(8,128)(2,1)} %copy-done.24) | copy-start | bytes 491524
  343.8 8.8 %copy-start.12 = (pred[128,4,2048]{0,2,1:T(8,128)(4,1)S(1)}, pred[128,4,2048]{0,2,1:T(8,128)(4,1)}, u32[]{:S(2)}) copy-start(pred[128,4,2048]{0,2,1:T(8,128)(4,1)} %get-tuple-element.27) | copy-start | bytes 3145732
  343.8 8.8 %copy-start.14 = (bf16[4,1,2,80,2048]{4,3,0,2,1:T(8,128)(2,1)S(1)}, bf16[4,1,2,80,2048]{4,3,0,2,1:T(8,128)(2,1)}, u32[]{:S(2)}) copy-start(bf16[4,1,2,80,2048]{4,3,0,2,1:T(8,128)(2,1)} %reshape.784) | copy-start | bytes 7864324
  352.6 13.6 %slice-start = ((s8[8388608]{0:T(1024)(128)(4,1)}), s8[4194304]{0:T(1024)(128)(4,1)S(1)}, s32[]{:S(2)}) async-start(s8[8388608]{0:T(1024)(128)(4,1)} %bitcast.327), calls=%async_computation.4 | async-start | bytes 8388608
  355.4 10.8 %copy-start.29 = (f32[128,4,4]{0,2,1:T(4,128)S(1)}, f32[128,4,4]{0,2,1:T(4,128)}, u32[]{:S(2)}) copy-start(f32[128,4,4]{0,2,1:T(4,128)} %copy-done.28) | copy-start | bytes 24580
  355.4 10.8 %copy-start.30 = (f32[128,4,4]{0,2,1:T(4,128)S(1)}, f32[128,4,4]{0,2,1:T(4,128)}, u32[]{:S(2)}) copy-start(f32[128,4,4]{0,2,1:T(4,128)} %fusion.15) | copy-start | bytes 24580
  355.4 10.8 %slice-start.1 = ((s8[8388608]{0:T(1024)(128)(4,1)}), s8[4194304]{0:T(1024)(128)(4,1)S(1)}, s32[]{:S(2)}) async-start(s8[8388608]{0:T(1024)(128)(4,1)} %bitcast.327), calls=%async_computation.5 | async-start | bytes 8388608
  355.4 10.8 %copy-start.16 = (pred[128,4,1024]{0,2,1:T(8,128)(4,1)S(1)}, pred[128,4,1024]{0,2,1:T(8,128)(4,1)}, u32[]{:S(2)}) copy-start(pred[128,4,1024]{0,2,1:T(8,128)(4,1)} %copy-done.15) | copy-start | bytes 1572868
  355.4 10.8 %copy-start.17 = (bf16[4,1,2,80,1024]{4,3,0,2,1:T(8,128)(2,1)S(1)}, bf16[4,1,2,80,1024]{4,3,0,2,1:T(8,128)(2,1)}, u32[]{:S(2)}) copy-start(bf16[4,1,2,80,1024]{4,3,0,2,1:T(8,128)(2,1)} %reshape.795) | copy-start | bytes 3932164
  380.1 5.8 copy-start.19
  399.4 0.7 copy-start.34
  399.4 196.4 %all-reduce.6.cloned.1.call-start = ((), (), s32[]{:S(2)}) async-start(), calls=%async_computation.3 | async-start | bytes 10485760
  483.7 2.3 copy-start.9
  519.0 0.7 copy-start.39
Sparse Core Ops, SparseCore 0:
  399.5 79.0 all-reduce.3
  519.1 76.6 all-reduce.5
